TPU v7x, 256 devices: a whole 4x4x8 slice. The times are simulated.
256 devices in a mesh: sens: 64 (over x, z_hi, y), grp: 4 (over z_lo, core).
Axes of the slice: x: 4, y: 4, z: 8 (z_hi: 4, z_lo: 2; z = z_hi * 2 + z_lo), core: 2. Of those that a mesh axis runs over, the one named last changes fastest.
Arguments:
- histories: bfloat16 [2048, 4096], P('sens', 'grp'), may hold values from -6 to 6
- bin_index: int32 [16], replicated, may hold values from 1 to 2047
- delays: int32 [2048, 4096], P('sens'), may hold values from 0 to 4095
- map_adjoint: float32 [4096], replicated, may hold values from -48 to 48
Outputs:
- history_adjoint: bfloat16 [2048, 4096], P('sens', 'grp')
Inputs may be any that keep to these rules, and one draw needn't show every extreme that they name: `delays`: each delay is already reduced modulo 4096.
All inputs are finite; a program needn't handle non-finite values.
Results may differ from a plain program's by a relative error of at most 0.0059.
Values may be sent and summed in bfloat16 or wider, within the bound.
No kernel may reach another device: no remote copies, remote signals or barrier semaphores. Data moves between devices by JAX's collectives and lax.ppermute only.
A program may use at most 64 MiB of HBM per device.

v0:
```python
import math
import jax
import jax.numpy as jnp
from jax import lax
from jax.sharding import PartitionSpec as P

NT = 4096
two_pi = 2.0 * math.pi


def transform_rows(first, count, bin_index, length):
    sample_times = first + lax.iota(jnp.int32, count)
    phase_index = sample_times[:, None] * bin_index[None, :] % length
    phase_angle = phase_index.astype(jnp.float32) * (two_pi / length)
    factor = 1.0 / math.sqrt(length)
    cosine = jnp.cos(phase_angle) * factor
    sine_part = -jnp.sin(phase_angle) * factor
    return jnp.concatenate([cosine, sine_part], 1).astype(jnp.bfloat16)


def circle_point(phase_index, length):
    eighth_bits = (length // 8).bit_length() - 1
    quarter = length // 4
    quadrant = phase_index >> eighth_bits + 1
    rest = phase_index & quarter - 1
    flip = rest >> eighth_bits & (rest != length // 8).astype(jnp.int32)
    folded = jnp.where(flip == 1, quarter - rest, rest)
    x = folded.astype(jnp.float32) * (two_pi / length)
    x2 = x * x
    sin_x = x * (1.0 + x2 * (-1.0 / 6.0 + x2 * (1.0 / 120.0 + x2 * (-1.0 / 5040.0))))
    cos_x = 1.0 + x2 * (-0.5 + x2 * (1.0 / 24.0 + x2 * (-1.0 / 720.0 + x2 * (1.0 / 40320.0))))
    swap = quadrant & 1 ^ flip == 1
    sine = jnp.where(swap, cos_x, sin_x)
    cosine = jnp.where(swap, sin_x, cos_x)
    sine = jnp.where(quadrant >= 2, -sine, sine)
    cosine = jnp.where((quadrant ^ quadrant >> 1) & 1 == 1, -cosine, cosine)
    return (cosine, sine)


def shifted(x, axis, shift):
    count = lax.axis_size(axis)
    return lax.ppermute(x, axis, [(j, (j + shift) % count) for j in range(count)])


def gather_stack(x, axis):
    count = lax.axis_size(axis)
    me = lax.axis_index(axis)
    stack = jnp.stack([x] + [shifted(x, axis, shift) for shift in range(1, count)])
    return stack[(me - jnp.arange(count)) % count]


def scatter_sum(x, axis):
    count = lax.axis_size(axis)
    lead = x.shape[:-1]
    parts = x.reshape(lead + (count, x.shape[-1] // count))
    parts = jnp.moveaxis(parts, -2, 0).reshape(count, -1)
    total = jnp.sum(lax.all_to_all(parts, axis, 0, 0, tiled=True), axis=0)
    return total.reshape(lead + (x.shape[-1] // count,))


def gather_last(x, axis):
    count = lax.axis_size(axis)
    copies = jnp.broadcast_to(x.reshape(1, -1), (count, x.size))
    joined = lax.all_to_all(copies, axis, 0, 0, tiled=True).reshape((count,) + x.shape)
    joined = jnp.moveaxis(joined, 0, -2)
    return joined.reshape(x.shape[:-1] + (count * x.shape[-1],))


def on_device(histories, bin_index, delays, map_adjoint):
    groups = lax.axis_size("grp")
    position = lax.axis_index("grp")
    bins = bin_index.shape[0]
    sensors = delays.shape[0] * lax.axis_size(SENS_AXES)
    steer_scale = 1.0 / math.sqrt(sensors)
    samples = histories.shape[1]
    scan_share = delays.shape[1] // groups
    transform = transform_rows(position * samples, samples, bin_index, NT)
    spectra = jnp.dot(histories, transform, preferred_element_type=jnp.float32)
    spectra = jnp.sum(gather_stack(spectra, "grp"), axis=0)
    real_t = spectra[:, :bins].T
    imag_t = spectra[:, bins:].T
    own_delays = lax.dynamic_slice_in_dim(delays, position * scan_share, scan_share, 1)
    own_weight = 2.0 * lax.dynamic_slice_in_dim(map_adjoint, position * scan_share, scan_share, 0)
    phase_index = bin_index[:, None, None] * own_delays[None, :, :] & NT - 1
    cosine, sine_part = lax.optimization_barrier(circle_point(phase_index, NT))
    steer_real = jnp.sum(real_t[:, :, None] * cosine - imag_t[:, :, None] * sine_part, axis=1)
    steer_imag = jnp.sum(real_t[:, :, None] * sine_part + imag_t[:, :, None] * cosine, axis=1)
    steered = jnp.stack([steer_real, steer_imag]) * steer_scale
    offset = 0
    for axis in SENS_AXES:
        offset = offset * lax.axis_size(axis) + lax.axis_index(axis)
    count = lax.axis_size(SENS_AXES)
    parts = steered.reshape(count, steered.size // count)
    width = parts.shape[1]
    chunk = jnp.sum(lax.all_to_all(parts, SENS_AXES, 0, 0, tiled=True), axis=0)
    start = offset * width % scan_share
    chunk = lax.dynamic_slice_in_dim(own_weight, start, width, 0) * chunk
    bar = lax.all_gather(chunk, SENS_AXES, tiled=True).reshape(steered.shape)
    bar_real = bar[0]
    bar_imag = bar[1]
    back_real = jnp.sum(bar_real[:, None, :] * cosine + bar_imag[:, None, :] * sine_part, axis=2)
    back_imag = jnp.sum(bar_imag[:, None, :] * cosine - bar_real[:, None, :] * sine_part, axis=2)
    back = jnp.concatenate([back_real.T, back_imag.T], 1) * steer_scale
    back = jnp.sum(gather_stack(back, "grp"), axis=0)
    adjoint = back.astype(jnp.bfloat16)
    local_part = lax.dot_general(
        adjoint, transform, (((1,), (1,)), ((), ())), preferred_element_type=jnp.float32
    )
    return local_part.astype(jnp.bfloat16)


SENS_AXES = ("sx", "sz", "sy")


def solution(mesh):
    sens_size = mesh.shape["sens"]
    side = round(sens_size ** (1.0 / 3.0))
    assert side**3 == sens_size
    fine = jax.sharding.Mesh(
        mesh.devices.reshape(side, side, side, mesh.shape["grp"]), SENS_AXES + ("grp",)
    )
    placed = (P(SENS_AXES, "grp"), P(), P(SENS_AXES, None), P())
    return jax.shard_map(
        on_device, mesh=fine, in_specs=placed, out_specs=P(SENS_AXES, "grp"), check_vma=False
    )
```

profile of v0, /device:TPU:1, one launch (start us, length us, event | category | flops | bytes accessed | tf_op | source)
XLA Modules:
  0.0 237.5 jit_solution(9495438284824854974)
XLA Ops:
  0.0 1.1 multiply_convert_fusion.1
  1.1 1.0 fusion.13
  2.0 3.0 %collective-permute-start = (f32[32,32]{0,1:T(8,128)S(1)}, f32[32,32]{0,1:T(8,128)S(1)}, u32[]{:S(2)}, u32[]{:S(2)}) collective-permute-start(f32[32,32]{0,1:T(8,128)S(1)} %bitcast.32), channel_id=1, source_target_pairs={{0,1},{1,2},{2,3},{3,0},{4,5},{5,6},{6,7},{7,4},{8,9},{9,10},{10,1... | collective-permute-start | bytes 12296 | tf_op jit(solution)/shard_map/ppermute | solution.py:42
  5.1 1.5 collective-permute-start.1
  6.6 0.0 collective-permute-start.2
  6.7 4.8 %negate_select_fusion = (f32[16,32,1024]{2,1,0:T(8,128)S(1)}, f32[16,32,1024]{2,1,0:T(8,128)}) fusion(s32[32,1024]{1,0:T(8,128)S(1)} %constant_dynamic-slice_fusion, s32[16]{0:T(128)} %param.5), kind=kLoop, calls=%fused_computation.2 | loop fusion | flops 22544384 | bytes 4325440 | tf_op jit(solution)/shard_map/jit(_where)/select_n | solution.py:35
  11.4 0.0 collective-permute-done.1
  11.5 0.6 gather_fusion
  12.1 3.1 %subtract_reduce_fusion.1 = (f32[16,1024]{1,0:T(8,128)S(1)}, f32[16,1024]{1,0:T(8,128)S(1)}) fusion(f32[16,32,1024]{2,1,0:T(8,128)S(1)} %get-tuple-element.8, f32[16,32,1024]{2,1,0:T(8,128)} %get-tuple-element.7, f32[16,32]{1,0:T(8,128)S(1)} %get-tuple-element.18, f32[16,32]{1,0:T(8,128)S(1)} %get-tuple-element.17), kind=kLoop, calls=%fused_computation.13 | loop fusion | flops 4161536 | bytes 4329472 | tf_op jit(solution)/shard_map/reduce_sum | solution.py:86
  15.2 0.8 mul.239
  16.0 12.6 %all-to-all-start = ((f32[64,1,512]{2,1,0:T(1,128)}), f32[64,1,512]{2,1,0:T(1,128)S(1)}, u32[]{:S(2)}, u32[]{:S(2)}) async-start(f32[64,1,512]{2,1,0:T(1,128)} %mul.239), calls=%async_computation | async-start | bytes 262144 | tf_op jit(solution)/shard_map/all_to_all | solution.py:95
  28.6 0.7 dynamic-slice_multiply_fusion
  29.3 10.7 %all-to-all-done = f32[64,1,512]{2,1,0:T(1,128)S(1)} async-done(((f32[64,1,512]{2,1,0:T(1,128)}), f32[64,1,512]{2,1,0:T(1,128)S(1)}, u32[]{:S(2)}, u32[]{:S(2)}) %all-to-all-start) | async-done | bytes 131104 | tf_op jit(solution)/shard_map/all_to_all | solution.py:95
  40.0 0.1 reduce_sum.66
  40.1 0.1 dynamic-slice_multiply_fusion.1
  40.2 157.9 %all-gather = f32[64,1,512]{2,1,0:T(1,128)S(1)} all-gather(f32[1,1,512]{2,1,0:T(1,128)S(1)} %bitcast.42), channel_id=1, replica_groups=mesh['sx'=4,'sz'=4,'sy'=4,'grp'=4] {'sx','sz','sy'}, dimensions={0}, use_global_device_ids=true | all-gather | bytes 133120 | tf_op jit(solution)/shard_map/all_gather | solution.py:98
  198.1 0.3 slice_reduce_fusion.1
  198.5 2.3 add_reduce_fusion
  200.8 31.0 %collective-permute-start.3 = (f32[32,32]{0,1:T(8,128)S(1)}, f32[32,32]{0,1:T(8,128)S(1)}, u32[]{:S(2)}, u32[]{:S(2)}) collective-permute-start(f32[32,32]{0,1:T(8,128)S(1)} %maximum_multiply_fusion.2), channel_id=1, source_target_pairs={{0,1},{1,2},{2,3},{3,0},{4,5},{5,6},{6,7},{7,4},{8,9},{9,10},{10,1... | collective-permute-start | bytes 12296 | tf_op jit(solution)/shard_map/ppermute | solution.py:42
  231.9 1.1 collective-permute-start.4
  232.9 1.5 collective-permute-done.4
  234.4 1.6 collective-permute-done.5
  236.1 0.6 gather_fusion.1
  236.7 0.8 convolution_convert_fusion
  (20 shorter events, 0.2 us)
Async XLA Ops:
  0.0 6.6 %copy-start = (s32[32,4096]{1,0:T(8,128)S(1)}, s32[32,4096]{1,0:T(8,128)}, u32[]{:S(2)}) copy-start(s32[32,4096]{1,0:T(8,128)} %param.6) | copy-start | bytes 1572868
  2.0 9.4 %collective-permute-start = (f32[32,32]{0,1:T(8,128)S(1)}, f32[32,32]{0,1:T(8,128)S(1)}, u32[]{:S(2)}, u32[]{:S(2)}) collective-permute-start(f32[32,32]{0,1:T(8,128)S(1)} %bitcast.32), channel_id=1, source_target_pairs={{0,1},{1,2},{2,3},{3,0},{4,5},{5,6},{6,7},{7,4},{8,9},{9,10},{10,1... | collective-permute-start | bytes 12296 | tf_op jit(solution)/shard_map/ppermute | solution.py:42
  5.1 6.4 %collective-permute-start.1 = (f32[32,32]{0,1:T(8,128)S(1)}, f32[32,32]{0,1:T(8,128)S(1)}, u32[]{:S(2)}, u32[]{:S(2)}) collective-permute-start(f32[32,32]{0,1:T(8,128)S(1)} %bitcast.33), channel_id=1, source_target_pairs={{0,2},{1,3},{2,0},{3,1},{4,6},{5,7},{6,4},{7,5},{8,10},{9,11},{10,... | collective-permute-start | bytes 12296 | tf_op jit(solution)/shard_map/ppermute | solution.py:42
  6.6 4.8 %collective-permute-start.2 = (f32[32,32]{0,1:T(8,128)S(1)}, f32[32,32]{0,1:T(8,128)S(1)}, u32[]{:S(2)}, u32[]{:S(2)}) collective-permute-start(f32[32,32]{0,1:T(8,128)S(1)} %bitcast.34), channel_id=1, source_target_pairs={{0,3},{1,0},{2,1},{3,2},{4,7},{5,4},{6,5},{7,6},{8,11},{9,8},{10,9... | collective-permute-start | bytes 12296 | tf_op jit(solution)/shard_map/ppermute | solution.py:42
  16.0 24.0 %all-to-all-start = ((f32[64,1,512]{2,1,0:T(1,128)}), f32[64,1,512]{2,1,0:T(1,128)S(1)}, u32[]{:S(2)}, u32[]{:S(2)}) async-start(f32[64,1,512]{2,1,0:T(1,128)} %mul.239), calls=%async_computation | async-start | bytes 262144 | tf_op jit(solution)/shard_map/all_to_all | solution.py:95
  200.8 32.1 %collective-permute-start.3 = (f32[32,32]{0,1:T(8,128)S(1)}, f32[32,32]{0,1:T(8,128)S(1)}, u32[]{:S(2)}, u32[]{:S(2)}) collective-permute-start(f32[32,32]{0,1:T(8,128)S(1)} %maximum_multiply_fusion.2), channel_id=1, source_target_pairs={{0,1},{1,2},{2,3},{3,0},{4,5},{5,6},{6,7},{7,4},{8,9},{9,10},{10,1... | collective-permute-start | bytes 12296 | tf_op jit(solution)/shard_map/ppermute | solution.py:42
  231.9 2.6 %collective-permute-start.4 = (f32[32,32]{0,1:T(8,128)S(1)}, f32[32,32]{0,1:T(8,128)S(1)}, u32[]{:S(2)}, u32[]{:S(2)}) collective-permute-start(f32[32,32]{0,1:T(8,128)S(1)} %maximum_multiply_fusion.2), channel_id=1, source_target_pairs={{0,2},{1,3},{2,0},{3,1},{4,6},{5,7},{6,4},{7,5},{8,10},{9,11},{10,... | collective-permute-start | bytes 12296 | tf_op jit(solution)/shard_map/ppermute | solution.py:42
  232.9 3.2 %collective-permute-start.5 = (f32[32,32]{0,1:T(8,128)S(1)}, f32[32,32]{0,1:T(8,128)S(1)}, u32[]{:S(2)}, u32[]{:S(2)}) collective-permute-start(f32[32,32]{0,1:T(8,128)S(1)} %maximum_multiply_fusion.2), channel_id=1, source_target_pairs={{0,3},{1,0},{2,1},{3,2},{4,7},{5,4},{6,5},{7,6},{8,11},{9,8},{10,9... | collective-permute-start | bytes 12296 | tf_op jit(solution)/shard_map/ppermute | solution.py:42
where the time goes:
time: 238 us
  blocking collectives  158 us (66%)
  starting transfers between devices  49.2 us (21%)
  waiting for transfers between devices  13.9 us (6%)
  other arithmetic  12.2 us (5%)
    all_gather x1, blocking collectives, on_device(): bar = lax.all_gather(chunk, SENS_AXES, tiled=True).reshape(steered.shape)  158 us
    ppermute x6, starting transfers between devices, shifted(): lax.ppermute(x, axis, [(j, (j + shift) % count) for j in range(count)])  36.7 us
    all_to_all x1, starting transfers between devices, on_device(): chunk = jnp.sum(lax.all_to_all(parts, SENS_AXES, 0, 0, tiled=True), axis=0)  12.6 us
    all_to_all x1, waiting for transfers between devices, on_device(): chunk = jnp.sum(lax.all_to_all(parts, SENS_AXES, 0, 0, tiled=True), axis=0)  10.7 us
    select_n x1, other arithmetic, circle_point(): sine = jnp.where(quadrant >= 2, -sine, sine)  4.77 us
  transfers between devices with their start and end apart: 7, of which 3 were waited for; matrix products, arithmetic and copies ran while one was open for 2% of the time, Pallas kernels for 0%

commit v1 on v0

--- a/solution.py
+++ b/solution.py
@@ -6,6 +6,13 @@
 
 NT = 4096
 two_pi = 2.0 * math.pi
+
+
+def _feed_target(tile_in):
+    cards = []
+    for _ in range(jax.lax.axis_size(SENS_AXES)):
+        cards.append(tile_in)
+    return jnp.concatenate(jax.lax.all_to_all(jnp.stack(cards, 0), SENS_AXES, 0, 0), 0)
 
 
 def transform_rows(first, count, bin_index, length):
@@ -95,7 +102,7 @@
     chunk = jnp.sum(lax.all_to_all(parts, SENS_AXES, 0, 0, tiled=True), axis=0)
     start = offset * width % scan_share
     chunk = lax.dynamic_slice_in_dim(own_weight, start, width, 0) * chunk
-    bar = lax.all_gather(chunk, SENS_AXES, tiled=True).reshape(steered.shape)
+    bar = _feed_target(chunk).reshape(steered.shape)
     bar_real = bar[0]
     bar_imag = bar[1]
     back_real = jnp.sum(bar_real[:, None, :] * cosine + bar_imag[:, None, :] * sine_part, axis=2)

time: 238 us -> 68.8 us (0.29)
  blocking collectives: 158 us -> 15.7 us
  starting transfers between devices: 49.2 us -> 22.3 us
    all_gather x1 -> x0, blocking collectives: 158 us -> none  [on_device(): bar = lax.all_gather(chunk, SENS_AXES, tiled=True).reshape(steered.shape)]
    ppermute x6, starting transfers between devices: 36.7 us -> 9.76 us  [shifted(): lax.ppermute(x, axis, [(j, (j + shift) % count) for j in range(count)])]
    all_to_all x0 -> x1, blocking collectives: none -> 15.7 us  [_feed_target(): jax.lax.all_to_all(jnp.stack(cards, 0), SENS_AXES, 0, 0)]
  transfers between devices with their start and end apart: 7 -> 7, of which waited for: 3 -> 4; matrix products, arithmetic and copies ran while one was open for 2% -> 8% of each run, Pallas kernels for 0% -> 0%
where the time goes in v1:
time: 68.8 us; the launch traced here: 68.4 us
  starting transfers between devices  22.3 us (32%)
  blocking collectives  15.7 us (23%)
  waiting for transfers between devices  13.9 us (20%)
  other arithmetic  12.2 us (18%)
  local copies, waits for them, and re-layouts  2.38 us (3%)
  matrix products  1.79 us (3%)
    all_to_all x1, blocking collectives, _feed_target(): jax.lax.all_to_all(jnp.stack(cards, 0), SENS_AXES, 0, 0)  15.7 us
    all_to_all x1, starting transfers between devices, on_device(): chunk = jnp.sum(lax.all_to_all(parts, SENS_AXES, 0, 0, tiled=True), axis=0)  12.6 us
    all_to_all x1, waiting for transfers between devices, on_device(): chunk = jnp.sum(lax.all_to_all(parts, SENS_AXES, 0, 0, tiled=True), axis=0)  10.7 us
    ppermute x6, starting transfers between devices, shifted(): lax.ppermute(x, axis, [(j, (j + shift) % count) for j in range(count)])  9.76 us
    select_n x1, other arithmetic, circle_point(): sine = jnp.where(quadrant >= 2, -sine, sine)  4.77 us
    ppermute x6, waiting for transfers between devices, shifted(): lax.ppermute(x, axis, [(j, (j + shift) % count) for j in range(count)])  3.16 us
    reduce_sum x1, other arithmetic, on_device(): jnp.sum(real_t[:, :, None] * cosine - imag_t[:, :, None] * sine_part, axi...  3.09 us
    reduce_sum x1, other arithmetic, on_device(): jnp.sum(bar_real[:, None, :] * cosine + bar_imag[:, None, :] * sine_part,...  2.32 us
  transfers between devices with their start and end apart: 7, of which 4 were waited for; matrix products, arithmetic and copies ran while one was open for 8% of the time, Pallas kernels for 0%

profile of v1, /device:TPU:1, one launch (start us, length us, event | category | flops | bytes accessed | tf_op | source)
XLA Modules:
  0.0 68.4 jit_solution(2975510089621858343)
XLA Ops:
  0.0 1.1 %multiply_convert_fusion.1 = (bf16[1024,16]{0,1:T(8,128)(2,1)S(1)}, bf16[1024,16]{0,1:T(8,128)(2,1)S(1)}) fusion(s32[16]{0:T(128)} %param.5, s32[1024]{0:T(1024)S(1)} %iota_add_fusion), kind=kLoop, calls=%fused_computation.42 | loop fusion | flops 311296 | bytes 69696 | tf_op jit(solution)/shard_map/convert
  1.1 1.0 %fusion.13 = f32[32,32]{1,0:T(8,128)S(1)} fusion(bf16[32,1024]{1,0:T(8,128)(2,1)} %param.4, bf16[1024,16]{0,1:T(8,128)(2,1)S(1)} %get-tuple-element.20, bf16[1024,16]{0,1:T(8,128)(2,1)S(1)} %get-tuple-element.19), kind=kOutput, calls=%fused_computation.43 | convolution fusion | flops 2228224 | bytes 135168 | tf_op jit(solution)/shard_map/dot_general | solution.py:85
  2.0 3.0 %collective-permute-start = (f32[32,32]{0,1:T(8,128)S(1)}, f32[32,32]{0,1:T(8,128)S(1)}, u32[]{:S(2)}, u32[]{:S(2)}) collective-permute-start(f32[32,32]{0,1:T(8,128)S(1)} %bitcast.31), channel_id=1, source_target_pairs={{0,1},{1,2},{2,3},{3,0},{4,5},{5,6},{6,7},{7,4},{8,9},{9,10},{10,1... | collective-permute-start | bytes 12296 | tf_op jit(solution)/shard_map/ppermute | solution.py:49
  5.1 1.5 %collective-permute-start.1 = (f32[32,32]{0,1:T(8,128)S(1)}, f32[32,32]{0,1:T(8,128)S(1)}, u32[]{:S(2)}, u32[]{:S(2)}) collective-permute-start(f32[32,32]{0,1:T(8,128)S(1)} %bitcast.32), channel_id=1, source_target_pairs={{0,2},{1,3},{2,0},{3,1},{4,6},{5,7},{6,4},{7,5},{8,10},{9,11},{10,... | collective-permute-start | bytes 12296 | tf_op jit(solution)/shard_map/ppermute | solution.py:49
  6.7 4.8 %negate_select_fusion = (f32[16,32,1024]{2,1,0:T(8,128)S(1)}, f32[16,32,1024]{2,1,0:T(8,128)}) fusion(s32[32,1024]{1,0:T(8,128)S(1)} %constant_dynamic-slice_fusion, s32[16]{0:T(128)} %param.5), kind=kLoop, calls=%fused_computation.2 | loop fusion | flops 22544384 | bytes 4325440 | tf_op jit(solution)/shard_map/jit(_where)/select_n | solution.py:42
  11.5 0.6 gather_fusion
  12.1 3.1 %subtract_reduce_fusion.1 = (f32[16,1024]{1,0:T(8,128)S(1)}, f32[16,1024]{1,0:T(8,128)S(1)}) fusion(f32[16,32,1024]{2,1,0:T(8,128)S(1)} %get-tuple-element.8, f32[16,32,1024]{2,1,0:T(8,128)} %get-tuple-element.7, f32[16,32]{1,0:T(8,128)S(1)} %get-tuple-element.18, f32[16,32]{1,0:T(8,128)S(1)} %get-tuple-element.17), kind=kLoop, calls=%fused_computation.13 | loop fusion | flops 4161536 | bytes 4329472 | tf_op jit(solution)/shard_map/reduce_sum | solution.py:93
  15.2 0.8 %mul.245 = f32[64,1,512]{2,1,0:T(1,128)} reshape(f32[2,16,1024]{2,1,0:T(8,128)S(1)} %maximum_multiply_fusion) | data formatting | bytes 262144 | tf_op jit(solution)/shard_map/mul | solution.py:95
  16.0 12.6 %all-to-all-start = ((f32[64,1,512]{2,1,0:T(1,128)}), f32[64,1,512]{2,1,0:T(1,128)S(1)}, u32[]{:S(2)}, u32[]{:S(2)}) async-start(f32[64,1,512]{2,1,0:T(1,128)} %mul.245), calls=%async_computation | async-start | bytes 262144 | tf_op jit(solution)/shard_map/all_to_all | solution.py:102
  28.6 0.7 %dynamic-slice_multiply_fusion = f32[1024]{0:T(1024)S(1)} fusion(f32[4096]{0:T(1024)} %param.7, s32[]{:T(128)S(6)} %select_n.63), kind=kLoop, calls=%fused_computation.51 | loop fusion | flops 1024 | bytes 8196 | tf_op jit(solution)/shard_map/mul | solution.py:90
  29.3 10.7 %all-to-all-done = f32[64,1,512]{2,1,0:T(1,128)S(1)} async-done(((f32[64,1,512]{2,1,0:T(1,128)}), f32[64,1,512]{2,1,0:T(1,128)S(1)}, u32[]{:S(2)}, u32[]{:S(2)}) %all-to-all-start) | async-done | bytes 131104 | tf_op jit(solution)/shard_map/all_to_all | solution.py:102
  40.0 0.1 reduce_sum.66
  40.1 0.1 dynamic-slice_multiply_fusion.1
  40.2 0.1 stack.34
  40.3 15.7 %all_to_all.12 = f32[64,1,512]{2,1,0:T(1,128)S(1)} all-to-all(f32[64,1,512]{2,1,0:T(1,128)S(1)} %stack.34), channel_id=1, replica_groups=mesh['sx'=4,'sz'=4,'sy'=4,'grp'=4] {'sx','sz','sy'}, dimensions={0} | all-to-all | bytes 262144 | tf_op jit(solution)/shard_map/all_to_all | solution.py:15
  55.9 0.3 slice_reduce_fusion.1
  56.3 2.3 %add_reduce_fusion = (f32[16,32]{1,0:T(8,128)S(1)}, f32[16,32]{1,0:T(8,128)S(1)}) fusion(f32[16,32,1024]{2,1,0:T(8,128)S(1)} %get-tuple-element.8, f32[16,32,1024]{2,1,0:T(8,128)} %get-tuple-element.7, f32[16,1024]{1,0:T(8,128)S(1)} %mul.236, f32[16,1024]{1,0:T(8,128)S(1)} %mul.233), kind=kLoop, calls=%fused_computation.11 | loop fusion | flops 4193280 | bytes 4329472 | tf_op jit(solution)/shard_map/reduce_sum | solution.py:108
  58.7 4.4 %collective-permute-start.3 = (f32[32,32]{0,1:T(8,128)S(1)}, f32[32,32]{0,1:T(8,128)S(1)}, u32[]{:S(2)}, u32[]{:S(2)}) collective-permute-start(f32[32,32]{0,1:T(8,128)S(1)} %maximum_multiply_fusion.2), channel_id=1, source_target_pairs={{0,1},{1,2},{2,3},{3,0},{4,5},{5,6},{6,7},{7,4},{8,9},{9,10},{10,1... | collective-permute-start | bytes 12296 | tf_op jit(solution)/shard_map/ppermute | solution.py:49
  63.1 0.8 %collective-permute-start.4 = (f32[32,32]{0,1:T(8,128)S(1)}, f32[32,32]{0,1:T(8,128)S(1)}, u32[]{:S(2)}, u32[]{:S(2)}) collective-permute-start(f32[32,32]{0,1:T(8,128)S(1)} %maximum_multiply_fusion.2), channel_id=1, source_target_pairs={{0,2},{1,3},{2,0},{3,1},{4,6},{5,7},{6,4},{7,5},{8,10},{9,11},{10,... | collective-permute-start | bytes 12296 | tf_op jit(solution)/shard_map/ppermute | solution.py:49
  63.9 0.1 collective-permute-done.3
  63.9 2.2 %collective-permute-done.4 = f32[32,32]{0,1:T(8,128)S(1)} collective-permute-done((f32[32,32]{0,1:T(8,128)S(1)}, f32[32,32]{0,1:T(8,128)S(1)}, u32[]{:S(2)}, u32[]{:S(2)}) %collective-permute-start.4) | collective-permute-done | bytes 4128 | tf_op jit(solution)/shard_map/ppermute | solution.py:49
  66.1 0.9 %collective-permute-done.5 = f32[32,32]{0,1:T(8,128)S(1)} collective-permute-done((f32[32,32]{0,1:T(8,128)S(1)}, f32[32,32]{0,1:T(8,128)S(1)}, u32[]{:S(2)}, u32[]{:S(2)}) %collective-permute-start.5) | collective-permute-done | bytes 4128 | tf_op jit(solution)/shard_map/ppermute | solution.py:49
  67.0 0.6 gather_fusion.1
  67.6 0.8 %convolution_convert_fusion = bf16[32,1024]{1,0:T(8,128)(2,1)} fusion(bf16[1024,16]{0,1:T(8,128)(2,1)S(1)} %get-tuple-element.20, bf16[1024,16]{0,1:T(8,128)(2,1)S(1)} %get-tuple-element.19, bf16[32,32]{0,1:T(8,128)(2,1)S(1)} %reduce_sum.69), kind=kOutput, calls=%fused_computation.26 | convolution fusion | flops 2260992 | bytes 133120 | tf_op jit(solution)/shard_map/dot_general | solution.py:113
  (21 shorter events, 0.2 us)
Async XLA Ops:
  0.0 6.6 %copy-start = (s32[32,4096]{1,0:T(8,128)S(1)}, s32[32,4096]{1,0:T(8,128)}, u32[]{:S(2)}) copy-start(s32[32,4096]{1,0:T(8,128)} %param.6) | copy-start | bytes 1572868
  2.0 9.4 %collective-permute-start = (f32[32,32]{0,1:T(8,128)S(1)}, f32[32,32]{0,1:T(8,128)S(1)}, u32[]{:S(2)}, u32[]{:S(2)}) collective-permute-start(f32[32,32]{0,1:T(8,128)S(1)} %bitcast.31), channel_id=1, source_target_pairs={{0,1},{1,2},{2,3},{3,0},{4,5},{5,6},{6,7},{7,4},{8,9},{9,10},{10,1... | collective-permute-start | bytes 12296 | tf_op jit(solution)/shard_map/ppermute | solution.py:49
  5.1 6.4 %collective-permute-start.1 = (f32[32,32]{0,1:T(8,128)S(1)}, f32[32,32]{0,1:T(8,128)S(1)}, u32[]{:S(2)}, u32[]{:S(2)}) collective-permute-start(f32[32,32]{0,1:T(8,128)S(1)} %bitcast.32), channel_id=1, source_target_pairs={{0,2},{1,3},{2,0},{3,1},{4,6},{5,7},{6,4},{7,5},{8,10},{9,11},{10,... | collective-permute-start | bytes 12296 | tf_op jit(solution)/shard_map/ppermute | solution.py:49
  6.6 4.8 %collective-permute-start.2 = (f32[32,32]{0,1:T(8,128)S(1)}, f32[32,32]{0,1:T(8,128)S(1)}, u32[]{:S(2)}, u32[]{:S(2)}) collective-permute-start(f32[32,32]{0,1:T(8,128)S(1)} %bitcast.33), channel_id=1, source_target_pairs={{0,3},{1,0},{2,1},{3,2},{4,7},{5,4},{6,5},{7,6},{8,11},{9,8},{10,9... | collective-permute-start | bytes 12296 | tf_op jit(solution)/shard_map/ppermute | solution.py:49
  16.0 24.0 %all-to-all-start = ((f32[64,1,512]{2,1,0:T(1,128)}), f32[64,1,512]{2,1,0:T(1,128)S(1)}, u32[]{:S(2)}, u32[]{:S(2)}) async-start(f32[64,1,512]{2,1,0:T(1,128)} %mul.245), calls=%async_computation | async-start | bytes 262144 | tf_op jit(solution)/shard_map/all_to_all | solution.py:102
  58.7 5.3 %collective-permute-start.3 = (f32[32,32]{0,1:T(8,128)S(1)}, f32[32,32]{0,1:T(8,128)S(1)}, u32[]{:S(2)}, u32[]{:S(2)}) collective-permute-start(f32[32,32]{0,1:T(8,128)S(1)} %maximum_multiply_fusion.2), channel_id=1, source_target_pairs={{0,1},{1,2},{2,3},{3,0},{4,5},{5,6},{6,7},{7,4},{8,9},{9,10},{10,1... | collective-permute-start | bytes 12296 | tf_op jit(solution)/shard_map/ppermute | solution.py:49
  63.1 3.1 %collective-permute-start.4 = (f32[32,32]{0,1:T(8,128)S(1)}, f32[32,32]{0,1:T(8,128)S(1)}, u32[]{:S(2)}, u32[]{:S(2)}) collective-permute-start(f32[32,32]{0,1:T(8,128)S(1)} %maximum_multiply_fusion.2), channel_id=1, source_target_pairs={{0,2},{1,3},{2,0},{3,1},{4,6},{5,7},{6,4},{7,5},{8,10},{9,11},{10,... | collective-permute-start | bytes 12296 | tf_op jit(solution)/shard_map/ppermute | solution.py:49
  63.9 3.2 %collective-permute-start.5 = (f32[32,32]{0,1:T(8,128)S(1)}, f32[32,32]{0,1:T(8,128)S(1)}, u32[]{:S(2)}, u32[]{:S(2)}) collective-permute-start(f32[32,32]{0,1:T(8,128)S(1)} %maximum_multiply_fusion.2), channel_id=1, source_target_pairs={{0,3},{1,0},{2,1},{3,2},{4,7},{5,4},{6,5},{7,6},{8,11},{9,8},{10,9... | collective-permute-start | bytes 12296 | tf_op jit(solution)/shard_map/ppermute | solution.py:49
